TPU v7x, 512 devices: a whole 4x8x8 slice. The times are simulated.
512 devices in a mesh: req: 64 (over x, y, core), tp: 8 (over z).
Axes of the slice: x: 4, y: 8, z: 8, core: 2. Of those that a mesh axis runs over, the one named last changes fastest.
Arguments:
- vit_context: bfloat16 [32768, 4096], P('req', 'tp'), may hold values from -6 to 6
- vision_residual: bfloat16 [32768, 4096], P('req', 'tp'), may hold values from -75 to 75
- out_weight: bfloat16 [4096, 4096], P('tp', 'req'), may hold values from -0.09375 to 0.09375
- layer_scale: float32 [4096], P('tp'), may hold values from 0.2 to 2
- prompt: bfloat16 [64, 256, 4096], P('req', None, 'tp'), may hold values from -75 to 75
- prompt_len: int32 [64], P('req'), may hold values from 128 to 256
- image_at: int32 [64], P('req'), may hold values from 0 to 128
- grid_sizes: int32 [128, 2], replicated, may hold values from 7 to 8, as said below
- image_owner: int32 [128], replicated, may hold values from 0 to 63, as said below
- norm_gain: float32 [4096], replicated, may hold values from 0.5 to 1.5
- qkv_weight: bfloat16 [4096, 6144], P('req', 'tp'), may hold values from -0.09375 to 0.09375
Outputs:
- qkv: bfloat16 [24576, 6144], P('req', 'tp')
Inputs may be any that keep to these rules, and one draw needn't show every extreme that they name: `image_owner`: each request owns exactly 2 images. `grid_sizes`: each side is 7 or 8; in every draw the images of some request are all 8 by 8, so that request has exactly 128 merged rows.
All inputs are finite; a program needn't handle non-finite values.
Results may differ from a plain program's by a relative error of at most 0.008.
Values may be sent and summed in bfloat16 or wider, within the bound.
No kernel may reach another device: no remote copies, remote signals or barrier semaphores. Data moves between devices by JAX's collectives and lax.ppermute only.
A program may use at most 64 MiB of HBM per device.

v0:
```python
import jax
import jax.numpy as jnp
from jax import lax
from jax.sharding import PartitionSpec as P

HEAD = 128
GROUP = 4
IMG_MAX = 128


def request_plan(grid_sizes, image_owner, requests):
    image_rows = grid_sizes[:, 0] * grid_sizes[:, 1]
    member = (image_owner[:, None] == jnp.arange(requests, dtype=jnp.int32)[None, :]).astype(
        jnp.int32
    )
    counts = jnp.sum(image_rows[:, None] * member, axis=0)
    starts = jnp.cumsum(counts) - counts
    return (counts, starts)


def rope_tables(count):
    half_size = HEAD // 2
    exponent = jnp.arange(half_size, dtype=jnp.float32) * (2.0 / HEAD)
    frequency = jnp.exp(-exponent * jnp.log(jnp.float32(500000.0)))
    angles = jnp.arange(count, dtype=jnp.float32)[:, None] * frequency[None, :]
    return (jnp.cos(angles), jnp.sin(angles))


def apply_rope(projected, cosine_table, sine_table):
    seq_rows = projected.shape[0]
    head_blocks = projected.reshape(seq_rows, -1, GROUP + 2, HEAD)
    turning = head_blocks[:, :, : GROUP + 1, :]
    first_half = turning[..., : HEAD // 2]
    second_half = turning[..., HEAD // 2 :]
    cosine_wide = cosine_table[:, None, None, :]
    sine_wide = sine_table[:, None, None, :]
    turned = jnp.concatenate(
        [
            first_half * cosine_wide - second_half * sine_wide,
            second_half * cosine_wide + first_half * sine_wide,
        ],
        axis=-1,
    )
    head_blocks = jnp.concatenate([turned, head_blocks[:, :, GROUP + 1 :, :]], axis=2)
    return head_blocks.reshape(seq_rows, -1)


def normalize(embedded, norm_gain):
    values = embedded.astype(jnp.float32)
    mean_square = jnp.mean(values * values, axis=-1, keepdims=True)
    return (values * lax.rsqrt(mean_square + 1e-05) * norm_gain[None, :]).astype(jnp.bfloat16)


def shards(
    vit_context,
    vision_residual,
    out_weight,
    layer_scale,
    prompt,
    prompt_len,
    image_at,
    grid_sizes,
    image_owner,
    norm_gain,
    qkv_weight,
):
    requests = lax.axis_size("req")
    device_index = lax.axis_index("req")
    feature_width = vit_context.shape[1]
    merged_context = jnp.mean(
        vit_context.astype(jnp.float32).reshape(-1, 4, feature_width), axis=1
    ).astype(jnp.bfloat16)
    merged_residual = jnp.mean(
        vision_residual.astype(jnp.float32).reshape(-1, 4, feature_width), axis=1
    )
    partial_value = jnp.dot(
        merged_context,
        lax.all_gather(out_weight, "req", axis=1, tiled=True),
        preferred_element_type=jnp.float32,
    )
    summed = lax.psum(partial_value.astype(jnp.bfloat16), "tp").astype(jnp.float32)
    own_share = lax.dynamic_slice_in_dim(
        summed, lax.axis_index("tp") * feature_width, feature_width, 1
    )
    merged = (merged_residual + layer_scale[None, :] * own_share).astype(jnp.bfloat16)
    merged_count = merged.shape[0]
    counts, starts = request_plan(grid_sizes, image_owner, requests)
    request_ends = starts + counts
    capacity = (IMG_MAX + requests - 1) // requests
    request_ids = jnp.arange(requests, dtype=jnp.int32)
    group_index = jnp.arange(merged_count, dtype=jnp.int32) * requests + device_index
    destination = jnp.sum((request_ends[None, :] <= group_index[:, None]).astype(jnp.int32), axis=1)
    owned_start = jnp.sum(
        jnp.where(destination[:, None] == request_ids[None, :], starts[None, :], 0), axis=1
    )
    target = destination * capacity + (group_index - owned_start) // requests
    usable = destination < requests
    send_slots = jnp.arange(requests * capacity, dtype=jnp.int32)
    placing = ((send_slots[:, None] == target[None, :]) & usable[None, :]).astype(jnp.bfloat16)
    outgoing = jnp.dot(placing, merged, preferred_element_type=jnp.float32).astype(jnp.bfloat16)
    arrived = lax.all_to_all(
        outgoing.reshape(requests, capacity, feature_width),
        "req",
        split_axis=0,
        concat_axis=0,
        tiled=True,
    )
    arrived = arrived.reshape(requests * capacity, feature_width)
    own_request = request_ids == device_index
    own_count = jnp.sum(jnp.where(own_request, counts, 0))
    own_start = jnp.sum(jnp.where(own_request, starts, 0))
    image_from = image_at[0]
    prompt_count = prompt_len[0]
    seq_slots = prompt.shape[1] + IMG_MAX
    slot_index = jnp.arange(seq_slots, dtype=jnp.int32)
    image_row = slot_index - image_from
    in_image = (image_row >= 0) & (image_row < own_count)
    is_live = slot_index < prompt_count + own_count
    from_prompt = is_live & jnp.logical_not(in_image)
    flat_index = (own_start + image_row) % requests * capacity + image_row // requests
    image_pick = ((flat_index[:, None] == send_slots[None, :]) & in_image[:, None]).astype(
        jnp.bfloat16
    )
    prompt_row = jnp.where(slot_index < image_from, slot_index, slot_index - own_count)
    prompt_ids = jnp.arange(prompt.shape[1], dtype=jnp.int32)
    prompt_pick = ((prompt_row[:, None] == prompt_ids[None, :]) & from_prompt[:, None]).astype(
        jnp.bfloat16
    )
    embedded = (
        jnp.dot(image_pick, arrived, preferred_element_type=jnp.float32)
        + jnp.dot(prompt_pick, prompt[0], preferred_element_type=jnp.float32)
    ).astype(jnp.bfloat16)
    gathered = lax.all_gather(embedded, "tp", axis=1, tiled=True)
    normed = normalize(gathered, norm_gain)
    projected = jnp.dot(
        normed,
        lax.all_gather(qkv_weight, "req", axis=0, tiled=True),
        preferred_element_type=jnp.float32,
    )
    cosine_table, sine_table = rope_tables(seq_slots)
    return apply_rope(projected, cosine_table, sine_table).astype(jnp.bfloat16)


def solution(mesh):
    in_specs = (
        P("req", "tp"),
        P("req", "tp"),
        P("tp", "req"),
        P("tp"),
        P("req", None, "tp"),
        P("req"),
        P("req"),
        P(),
        P(),
        P(),
        P("req", "tp"),
    )
    out_specs = P("req", "tp")
    return jax.shard_map(shards, mesh=mesh, in_specs=in_specs, out_specs=out_specs, check_vma=False)
```

profile of v0, /device:TPU:1, one launch (start us, length us, event | category | flops | bytes accessed | tf_op | source)
XLA Modules:
  0.0 352.9 jit_solution(7770393168710454331)
XLA Ops:
  6.5 0.7 all-gather.4.cloned.1.call-update
  7.3 1.4 reshape.205
  8.7 0.6 reduce_sum.78
  9.3 0.8 multiply_bitcast_fusion
  10.1 91.0 %all-gather.4.cloned.1.call-done = bf16[512,4096]{0,1:T(8,128)(2,1)} async-done(((bf16[512,64]{0,1:T(8,128)(2,1)}), bf16[512,4096]{0,1:T(8,128)(2,1)}) %all-gather.4.cloned.1.call-update) | async-done | bytes 4194320 | tf_op jit(solution)/shard_map/all_gather | solution.py:78
  101.1 4.6 %convolution_convert_fusion = bf16[128,4096]{1,0:T(8,128)(2,1)} fusion(bf16[512,4096]{0,1:T(8,128)(2,1)} %all-gather.4.cloned.1.call-done, f32[128,512]{1,0:T(8,128)S(1)} %reduce_sum.78), kind=kOutput, calls=%fused_computation.5 | convolution fusion | flops 537526272 | bytes 5505024 | tf_op jit(solution)/shard_map/dot_general | solution.py:76
  105.7 0.1 select_reduce_fusion.1
  105.8 0.1 copy.16
  105.9 0.1 reduce-window.7
  106.0 0.1 reduce
  106.2 0.3 reshape.203
  106.5 0.6 reduce_sum.77
  107.2 0.1 convert_reduce_fusion
  107.3 0.7 fusion.38
  108.0 0.1 select_reduce_fusion
  108.1 73.3 %all-reduce.2.cloned.1.call-done = bf16[128,4096]{1,0:T(8,128)(2,1)} async-done(((bf16[128,4096]{1,0:T(8,128)(2,1)}), bf16[128,4096]{1,0:T(8,128)(2,1)}) %all-reduce.2.cloned.1.call-update) | async-done | bytes 1048592 | tf_op jit(solution)/shard_map/psum | solution.py:81
  181.4 1.1 convolution_convert_fusion.1
  182.5 0.7 reshape.199
  183.3 14.2 %all-to-all-start = ((bf16[64,2,512]{2,1,0:T(2,128)(2,1)}), bf16[64,2,512]{2,1,0:T(2,128)(2,1)S(1)}, u32[]{:S(2)}, u32[]{:S(2)}) async-start(bf16[64,2,512]{2,1,0:T(2,128)(2,1)} %reshape.199), calls=%async_computation | async-start | bytes 262144 | tf_op jit(solution)/shard_map/all_to_all | solution.py:101
  199.3 0.6 fusion.37
  199.9 1.3 fusion.30
  201.2 6.6 %all-to-all-done = bf16[64,2,512]{2,1,0:T(2,128)(2,1)S(1)} async-done(((bf16[64,2,512]{2,1,0:T(2,128)(2,1)}), bf16[64,2,512]{2,1,0:T(2,128)(2,1)S(1)}, u32[]{:S(2)}, u32[]{:S(2)}) %all-to-all-start) | async-done | bytes 131104 | tf_op jit(solution)/shard_map/all_to_all | solution.py:101
  207.9 0.3 fusion.14
  208.2 1.1 fusion.7
  209.3 0.5 all-gather.8.cloned.1.call-update
  209.9 0.4 fusion.21
  210.3 40.0 %all-gather.6.cloned.1.call-done = bf16[384,4096]{1,0:T(8,128)(2,1)} async-done(((bf16[384,512]{1,0:T(8,128)(2,1)}), bf16[384,4096]{1,0:T(8,128)(2,1)}) %all-gather.6.cloned.1.call-update) | async-done | bytes 3145744 | tf_op jit(solution)/shard_map/all_gather | solution.py:133
  250.3 2.6 fusion
  252.9 85.4 %all-gather.8.cloned.1.call-done = bf16[4096,768]{1,0:T(8,128)(2,1)} async-done(((bf16[64,768]{1,0:T(8,128)(2,1)}), bf16[4096,768]{1,0:T(8,128)(2,1)}) %all-gather.8.cloned.1.call-update) | async-done | bytes 6291472 | tf_op jit(solution)/shard_map/all_gather | solution.py:137
  338.3 6.7 %fusion.3 = f32[384,768]{0,1:T(8,128)S(1)} fusion(bf16[4096,768]{1,0:T(8,128)(2,1)} %all-gather.8.cloned.1.call-done, bf16[384,4096]{1,0:T(8,128)(2,1)} %all-gather.6.cloned.1.call-done, f32[4096]{0:T(1024)S(1)} %copy-done.3, f32[384]{0:T(512)S(1)} %add_rsqrt_fusion), kind=kOutput, calls=%fused_computation.6 | convolution fusion | flops 2422210560 | bytes 10634752 | tf_op jit(solution)/shard_map/dot_general | solution.py:135
  345.0 0.1 subtract_convert_fusion
  345.2 1.1 copy.18
  (24 shorter events, 0.4 us)
Async XLA Ops:
  6.5 201.7 %copy-start = (bf16[1,256,512]{2,1,0:T(8,128)(2,1)S(1)}, bf16[1,256,512]{2,1,0:T(8,128)(2,1)}, u32[]{:S(2)}) copy-start(bf16[1,256,512]{2,1,0:T(8,128)(2,1)} %param.15) | copy-start | bytes 786436
  6.5 94.5 %all-gather.4.cloned.1.call-start = ((), (), s32[]{:S(2)}) async-start(), calls=%async_computation.1 | async-start | bytes 4259840 | tf_op jit(solution)/shard_map/all_gather | solution.py:78
  7.3 174.2 %all-reduce.2.cloned.1.call-start = ((), (), s32[]{:S(2)}) async-start(), calls=%async_computation.2 | async-start | bytes 2097152 | tf_op jit(solution)/shard_map/psum | solution.py:81
  8.7 97.0 %copy-start.4 = (s32[128]{0:T(128)S(1)}, s32[128]{0:T(128)}, u32[]{:S(2)}) copy-start(s32[128]{0:T(128)} %param.19) | copy-start | bytes 1540
  8.7 97.5 %copy-start.1 = (bf16[512,512]{1,0:T(8,128)(2,1)S(1)}, bf16[512,512]{1,0:T(8,128)(2,1)}, u32[]{:S(2)}) copy-start(bf16[512,512]{1,0:T(8,128)(2,1)} %param.12) | copy-start | bytes 1572868
  10.1 171.3 %copy-start.2 = (f32[512]{0:T(512)S(1)}, f32[512]{0:T(512)}, u32[]{:S(2)}) copy-start(f32[512]{0:T(512)} %param.14) | copy-start | bytes 6148
  106.5 231.8 %copy-start.3 = (f32[4096]{0:T(1024)S(1)}, f32[4096]{0:T(1024)}, u32[]{:S(2)}) copy-start(f32[4096]{0:T(1024)} %param.20) | copy-start | bytes 49156
  183.3 24.5 %all-to-all-start = ((bf16[64,2,512]{2,1,0:T(2,128)(2,1)}), bf16[64,2,512]{2,1,0:T(2,128)(2,1)S(1)}, u32[]{:S(2)}, u32[]{:S(2)}) async-start(bf16[64,2,512]{2,1,0:T(2,128)(2,1)} %reshape.199), calls=%async_computation | async-start | bytes 262144 | tf_op jit(solution)/shard_map/all_to_all | solution.py:101
  197.4 52.9 %all-gather.6.cloned.1.call-start = ((), (), s32[]{:S(2)}) async-start(), calls=%async_computation.3 | async-start | bytes 3538944 | tf_op jit(solution)/shard_map/all_gather | solution.py:133
  209.3 129.0 %all-gather.8.cloned.1.call-start = ((), (), s32[]{:S(2)}) async-start(), calls=%async_computation.4 | async-start | bytes 6389760 | tf_op jit(solution)/shard_map/all_gather | solution.py:137
Sparse Core Ops, SparseCore 0:
  10.7 90.2 all-gather.3
  105.8 75.5 all-reduce.1
  209.4 40.8 all-gather.5
  253.5 84.7 all-gather.7
where the time goes:
time: 353 us
  waiting for transfers between devices  298 us (84%)
  between operations  15.2 us (4%)
  starting transfers between devices  14.3 us (4%)
  matrix products  13.8 us (4%)
  other arithmetic  8.27 us (2%)
  local copies, waits for them, and re-layouts  3.69 us (1%)
    all_gather x1, waiting for transfers between devices, shards(): lax.all_gather(out_weight, 'req', axis=1, tiled=True)  91 us
    all_gather x1, waiting for transfers between devices, shards(): lax.all_gather(qkv_weight, 'req', axis=0, tiled=True)  85.4 us
    psum x1, waiting for transfers between devices, shards(): lax.psum(partial_value.astype(jnp.bfloat16), 'tp').astype(jnp.float32)  73.3 us
    all_gather x1, waiting for transfers between devices, shards(): gathered = lax.all_gather(embedded, 'tp', axis=1, tiled=True)  40 us
    all_to_all x1, starting transfers between devices, shards(): lax.all_to_all(outgoing.reshape(requests, capacity, feature_width), 'req'...  14.2 us
  transfers between devices with their start and end apart: 5, of which 5 were waited for; matrix products, arithmetic and copies ran while one was open for 3% of the time, Pallas kernels for 0%

commit v1 on v0

--- a/solution.py
+++ b/solution.py
@@ -75,7 +75,9 @@
     )
     partial_value = jnp.dot(
         merged_context,
-        lax.all_gather(out_weight, "req", axis=1, tiled=True),
+        jnp.concatenate(
+            lax.all_to_all(jnp.stack([out_weight] * lax.axis_size("req")), "req", 0, 0), axis=1
+        ),
         preferred_element_type=jnp.float32,
     )
     summed = lax.psum(partial_value.astype(jnp.bfloat16), "tp").astype(jnp.float32)

time: 353 us -> 373 us (1.057)
  starting transfers between devices: 14.3 us -> 26.3 us
  waiting for transfers between devices: 298 us -> 303 us
    all_to_all x0 -> x1, waiting for transfers between devices: none -> 94.9 us  [shards(): lax.all_to_all(jnp.stack([out_weight] * lax.axis_size('req')), 'req', 0, 0)]
    all_gather x1 -> x0, waiting for transfers between devices: 91 us -> none  [shards(): lax.all_gather(out_weight, 'req', axis=1, tiled=True)]
    all_to_all x0 -> x1, starting transfers between devices: none -> 12 us  [shards(): lax.all_to_all(jnp.stack([out_weight] * lax.axis_size('req')), 'req', 0, 0)]
  transfers between devices with their start and end apart: 5 -> 5, of which waited for: 5 -> 5; matrix products, arithmetic and copies ran while one was open for 3% -> 2% of each run, Pallas kernels for 0% -> 0%
where the time goes in v1:
time: 373 us; the launch traced here: 372 us
  waiting for transfers between devices  303 us (81%)
  starting transfers between devices  26.3 us (7%)
  between operations  15.2 us (4%)
  matrix products  13.8 us (4%)
  other arithmetic  7.52 us (2%)
  local copies, waits for them, and re-layouts  6.01 us (2%)
    all_to_all x1, waiting for transfers between devices, shards(): lax.all_to_all(jnp.stack([out_weight] * lax.axis_size('req')), 'req', 0, 0)  94.9 us
    all_gather x1, waiting for transfers between devices, shards(): lax.all_gather(qkv_weight, 'req', axis=0, tiled=True)  85.5 us
    psum x1, waiting for transfers between devices, shards(): lax.psum(partial_value.astype(jnp.bfloat16), 'tp').astype(jnp.float32)  75.8 us
    all_gather x1, waiting for transfers between devices, shards(): gathered = lax.all_gather(embedded, 'tp', axis=1, tiled=True)  39.9 us
    all_to_all x1, starting transfers between devices, shards(): lax.all_to_all(outgoing.reshape(requests, capacity, feature_width), 'req'...  14.2 us
    all_to_all x1, starting transfers between devices, shards(): lax.all_to_all(jnp.stack([out_weight] * lax.axis_size('req')), 'req', 0, 0)  12 us
  transfers between devices with their start and end apart: 5, of which 5 were waited for; matrix products, arithmetic and copies ran while one was open for 2% of the time, Pallas kernels for 0%

profile of v1, /device:TPU:1, one launch (start us, length us, event | category | flops | bytes accessed | tf_op | source)
XLA Modules:
  0.0 372.3 jit_solution(16158290020068252007)
XLA Ops:
  6.5 3.4 stack.2
  9.9 12.0 %all-to-all-start = ((bf16[64,512,64]{1,2,0:T(8,128)(2,1)}), bf16[64,512,64]{1,2,0:T(8,128)(2,1)}, u32[]{:S(2)}, u32[]{:S(2)}) async-start(bf16[64,512,64]{1,2,0:T(8,128)(2,1)} %stack.2), calls=%async_computation | async-start | bytes 8388608 | tf_op jit(solution)/shard_map/all_to_all | solution.py:79
  22.0 0.3 reshape.215
  22.4 0.6 reduce_sum.78
  23.0 94.9 %all-to-all-done = bf16[64,512,64]{1,2,0:T(8,128)(2,1)} async-done(((bf16[64,512,64]{1,2,0:T(8,128)(2,1)}), bf16[64,512,64]{1,2,0:T(8,128)(2,1)}, u32[]{:S(2)}, u32[]{:S(2)}) %all-to-all-start) | async-done | bytes 4194336 | tf_op jit(solution)/shard_map/all_to_all | solution.py:79
  117.9 4.7 %convolution_convert_fusion = bf16[128,4096]{1,0:T(8,128)(2,1)} fusion(bf16[512,4096]{0,1:T(8,128)(2,1)} %bitcast.4, f32[128,512]{1,0:T(8,128)S(1)} %reduce_sum.78), kind=kOutput, calls=%fused_computation.5 | convolution fusion | flops 537526272 | bytes 5505024 | tf_op jit(solution)/shard_map/dot_general | solution.py:76
  122.6 0.1 select_reduce_fusion.1
  122.7 0.1 copy.17
  122.8 0.1 reduce-window.7
  122.9 0.1 reduce
  123.0 0.3 reshape.213
  123.4 0.6 reduce_sum.77
  124.0 0.1 convert_reduce_fusion
  124.1 0.7 fusion.38
  124.8 0.1 select_reduce_fusion
  124.9 75.8 %all-reduce.2.cloned.1.call-done = bf16[128,4096]{1,0:T(8,128)(2,1)} async-done(((bf16[128,4096]{1,0:T(8,128)(2,1)}), bf16[128,4096]{1,0:T(8,128)(2,1)}) %all-reduce.2.cloned.1.call-update) | async-done | bytes 1048592 | tf_op jit(solution)/shard_map/psum | solution.py:83
  200.7 1.1 convolution_convert_fusion.1
  201.8 0.7 reshape.209
  202.5 14.2 %all-to-all-start.1 = ((bf16[64,2,512]{2,1,0:T(2,128)(2,1)}), bf16[64,2,512]{2,1,0:T(2,128)(2,1)S(1)}, u32[]{:S(2)}, u32[]{:S(2)}) async-start(bf16[64,2,512]{2,1,0:T(2,128)(2,1)} %reshape.209), calls=%async_computation.1 | async-start | bytes 262144 | tf_op jit(solution)/shard_map/all_to_all | solution.py:103
  218.6 0.6 fusion.37
  219.2 1.3 fusion.30
  220.4 6.6 %all-to-all-done.1 = bf16[64,2,512]{2,1,0:T(2,128)(2,1)S(1)} async-done(((bf16[64,2,512]{2,1,0:T(2,128)(2,1)}), bf16[64,2,512]{2,1,0:T(2,128)(2,1)S(1)}, u32[]{:S(2)}, u32[]{:S(2)}) %all-to-all-start.1) | async-done | bytes 131104 | tf_op jit(solution)/shard_map/all_to_all | solution.py:103
  227.1 0.3 fusion.14
  227.5 1.1 fusion.7
  228.6 0.7 all-gather.5.cloned.1.call-update
  229.3 0.4 fusion.21
  229.7 39.9 %all-gather.3.cloned.1.call-done = bf16[384,4096]{1,0:T(8,128)(2,1)} async-done(((bf16[384,512]{1,0:T(8,128)(2,1)}), bf16[384,4096]{1,0:T(8,128)(2,1)}) %all-gather.3.cloned.1.call-update) | async-done | bytes 3145744 | tf_op jit(solution)/shard_map/all_gather | solution.py:135
  269.6 2.6 fusion
  272.2 85.5 %all-gather.5.cloned.1.call-done = bf16[4096,768]{1,0:T(8,128)(2,1)} async-done(((bf16[64,768]{1,0:T(8,128)(2,1)}), bf16[4096,768]{1,0:T(8,128)(2,1)}) %all-gather.5.cloned.1.call-update) | async-done | bytes 6291472 | tf_op jit(solution)/shard_map/all_gather | solution.py:139
  357.7 6.7 %fusion.3 = f32[384,768]{0,1:T(8,128)S(1)} fusion(bf16[4096,768]{1,0:T(8,128)(2,1)} %all-gather.5.cloned.1.call-done, bf16[384,4096]{1,0:T(8,128)(2,1)} %all-gather.3.cloned.1.call-done, f32[4096]{0:T(1024)S(1)} %copy-done.4, f32[384]{0:T(512)S(1)} %add_rsqrt_fusion), kind=kOutput, calls=%fused_computation.6 | convolution fusion | flops 2422210560 | bytes 10634752 | tf_op jit(solution)/shard_map/dot_general | solution.py:137
  364.5 0.1 subtract_convert_fusion
  364.7 1.1 copy.19
  (28 shorter events, 0.4 us)
Async XLA Ops:
  6.5 220.9 %copy-start = (bf16[1,256,512]{2,1,0:T(8,128)(2,1)S(1)}, bf16[1,256,512]{2,1,0:T(8,128)(2,1)}, u32[]{:S(2)}) copy-start(bf16[1,256,512]{2,1,0:T(8,128)(2,1)} %param.15) | copy-start | bytes 786436
  9.9 12.1 %copy-start.1 = (bf16[512,512]{1,0:T(8,128)(2,1)S(1)}, bf16[512,512]{1,0:T(8,128)(2,1)}, u32[]{:S(2)}) copy-start(bf16[512,512]{1,0:T(8,128)(2,1)} %param.11) | copy-start | bytes 1572868
  9.9 13.1 %copy-start.5 = (s32[128,2]{0,1:T(2,128)S(1)}, s32[128,2]{0,1:T(2,128)}, u32[]{:S(2)}) copy-start(s32[128,2]{0,1:T(2,128)} %param.18) | copy-start | bytes 3076
  9.9 108.0 %all-to-all-start = ((bf16[64,512,64]{1,2,0:T(8,128)(2,1)}), bf16[64,512,64]{1,2,0:T(8,128)(2,1)}, u32[]{:S(2)}, u32[]{:S(2)}) async-start(bf16[64,512,64]{1,2,0:T(8,128)(2,1)} %stack.2), calls=%async_computation | async-start | bytes 8388608 | tf_op jit(solution)/shard_map/all_to_all | solution.py:79
  21.9 178.8 %all-reduce.2.cloned.1.call-start = ((), (), s32[]{:S(2)}) async-start(), calls=%async_computation.2 | async-start | bytes 2097152 | tf_op jit(solution)/shard_map/psum | solution.py:83
  22.3 100.2 %copy-start.6 = (s32[128]{0:T(128)S(1)}, s32[128]{0:T(128)}, u32[]{:S(2)}) copy-start(s32[128]{0:T(128)} %param.19) | copy-start | bytes 1540
  22.3 100.7 %copy-start.2 = (bf16[512,512]{1,0:T(8,128)(2,1)S(1)}, bf16[512,512]{1,0:T(8,128)(2,1)}, u32[]{:S(2)}) copy-start(bf16[512,512]{1,0:T(8,128)(2,1)} %param.12) | copy-start | bytes 1572868
  117.9 82.8 %copy-start.3 = (f32[512]{0:T(512)S(1)}, f32[512]{0:T(512)}, u32[]{:S(2)}) copy-start(f32[512]{0:T(512)} %param.14) | copy-start | bytes 6148
  123.3 234.4 %copy-start.4 = (f32[4096]{0:T(1024)S(1)}, f32[4096]{0:T(1024)}, u32[]{:S(2)}) copy-start(f32[4096]{0:T(1024)} %param.20) | copy-start | bytes 49156
  202.5 24.5 %all-to-all-start.1 = ((bf16[64,2,512]{2,1,0:T(2,128)(2,1)}), bf16[64,2,512]{2,1,0:T(2,128)(2,1)S(1)}, u32[]{:S(2)}, u32[]{:S(2)}) async-start(bf16[64,2,512]{2,1,0:T(2,128)(2,1)} %reshape.209), calls=%async_computation.1 | async-start | bytes 262144 | tf_op jit(solution)/shard_map/all_to_all | solution.py:103
  216.7 52.9 %all-gather.3.cloned.1.call-start = ((), (), s32[]{:S(2)}) async-start(), calls=%async_computation.3 | async-start | bytes 3538944 | tf_op jit(solution)/shard_map/all_gather | solution.py:135
  228.6 129.2 %all-gather.5.cloned.1.call-start = ((), (), s32[]{:S(2)}) async-start(), calls=%async_computation.4 | async-start | bytes 6389760 | tf_op jit(solution)/shard_map/all_gather | solution.py:139
Sparse Core Ops, SparseCore 0:
  122.7 77.9 all-reduce.1
  228.7 40.8 all-gather.2
  272.9 84.7 all-gather.4
